TPU v7x, 32 devices: a whole 2x2x4 slice. The times are simulated.
32 devices in a mesh: row: 8 (over z, y), rep: 4 (over x, core).
Axes of the slice: x: 2, y: 2, z: 4, core: 2. Of those that a mesh axis runs over, the one named last changes fastest.
Arguments:
- features: bfloat16 [2048, 256], P('row'), may hold values from -6 to 6
- cotangent: bfloat16 [2048, 256], P('row'), may hold values from -0.3125 to 0.3125
- weight_one: bfloat16 [256, 256], replicated, may hold values from -0.375 to 0.375
- weight_two: bfloat16 [256, 256], replicated, may hold values from -0.375 to 0.375
- block_index: int32 [8, 4, 2, 4], P('row', 'rep'), may hold values from 0 to 15, as said below
- block_count: int32 [8, 4, 2], P('row', 'rep'), may hold values from 0 to 4
- block_values: bfloat16 [8, 4, 2, 4, 128, 128], P('row', 'rep'), as said below
Outputs:
- logits: bfloat16 [2048, 256], P(('row', 'rep'))
- grad_one: float32 [256, 256], replicated
- grad_two: float32 [256, 256], replicated
Inputs may be any that keep to these rules, and one draw needn't show every extreme that they name: block_index[i, j, a, s] lies in [j * 4, (j + 1) * 4); for s < block_count[i, j, a] the entries rise strictly; later entries equal j * 4 and are not part of A. `block_values`: A is symmetric: block (r, c) is listed exactly when block (c, r) is, and its entries are the transpose of those of block (c, r). Entries are normal with standard deviation (0.5 * 128 * 16) ** -0.5, cut at five such deviations; blocks on the diagonal are symmetric.
All inputs are finite; a program needn't handle non-finite values.
Results may differ from a plain program's by a relative error of at most 0.0059.
Values may be sent and summed in bfloat16 or wider, within the bound.
No kernel may reach another device: no remote copies, remote signals or barrier semaphores. Data moves between devices by JAX's collectives and lax.ppermute only.
A program may use at most 64 MiB of HBM per device.

v0:
```python
import jax
import jax.numpy as jnp
from jax import lax
from jax.sharding import PartitionSpec as P


def broadcast(array, axis, root):
    mine = lax.axis_index(axis) == root
    return lax.psum(jnp.where(mine, array, jnp.zeros_like(array)), axis)


def aggregate(source, block_index, block_count, block_values):
    copies = lax.axis_size("rep")
    sections = lax.axis_size("row") // copies
    copy_index = lax.axis_index("rep")
    node_rows, feature_width = source.shape
    block_rows = block_values.shape[2]
    slot_count = block_values.shape[3]
    block_side = block_values.shape[-1]

    def fetch(state_unused, section_index):
        panel = broadcast(source, "row", copy_index * sections + section_index)
        return (state_unused, panel)

    state_unused, panels = lax.scan(fetch, jnp.int32(0), jnp.arange(sections, dtype=jnp.int32))
    panels = panels.reshape(sections * block_rows, block_side, feature_width)
    columns = block_index[0, 0] - copy_index * slot_count
    live_slots = jnp.arange(slot_count, dtype=jnp.int32)[None, :] < block_count[0, 0][:, None]
    picked = jnp.take(panels, columns.reshape(-1), axis=0).reshape(
        block_rows, slot_count, block_side, feature_width
    )
    picked = jnp.where(live_slots[:, :, None, None], picked, jnp.zeros((), picked.dtype))
    partial_value = lax.dot_general(
        block_values[0, 0],
        picked,
        (((1, 3), (1, 2)), ((0,), (0,))),
        preferred_element_type=jnp.float32,
    )
    partial_value = partial_value.reshape(node_rows, feature_width)
    result = lax.psum(partial_value, "rep")
    return result


def shards(features, cotangent, weight_one, weight_two, block_index, block_count, block_values):
    copies = lax.axis_size("rep")
    copy_index = lax.axis_index("rep")
    node_rows = features.shape[0]
    share_rows = node_rows // copies
    first_row = copy_index * share_rows

    def own_rows(array):
        return lax.dynamic_slice_in_dim(array, first_row, share_rows, 0)

    agg_one = aggregate(features, block_index, block_count, block_values).astype(jnp.bfloat16)
    pre_one = jnp.dot(agg_one, weight_one, preferred_element_type=jnp.float32)
    hidden = jax.nn.silu(pre_one).astype(jnp.bfloat16)
    agg_two = aggregate(hidden, block_index, block_count, block_values).astype(jnp.bfloat16)
    agg_two_own = own_rows(agg_two)
    logits = jnp.dot(agg_two_own, weight_two, preferred_element_type=jnp.float32).astype(
        jnp.bfloat16
    )
    cotangent_own = own_rows(cotangent)
    grad_two = lax.dot_general(
        agg_two_own, cotangent_own, (((0,), (0,)), ((), ())), preferred_element_type=jnp.float32
    )
    grad_two = lax.psum(grad_two, ("row", "rep"))
    back_signal = lax.dot_general(
        cotangent, weight_two, (((1,), (1,)), ((), ())), preferred_element_type=jnp.float32
    ).astype(jnp.bfloat16)
    carried = aggregate(back_signal, block_index, block_count, block_values)
    carried = own_rows(carried)
    pre_own = own_rows(pre_one)
    agg_one_own = own_rows(agg_one)
    gate_value = jax.nn.sigmoid(pre_own)
    pre_grad = (carried * (gate_value + pre_own * gate_value * (1.0 - gate_value))).astype(
        jnp.bfloat16
    )
    grad_one = lax.dot_general(
        agg_one_own, pre_grad, (((0,), (0,)), ((), ())), preferred_element_type=jnp.float32
    )
    grad_one = lax.psum(grad_one, ("row", "rep"))
    return (logits, grad_one, grad_two)


def solution(mesh):
    in_specs = (
        P("row", None),
        P("row", None),
        P(),
        P(),
        P("row", "rep", None, None),
        P("row", "rep", None),
        P("row", "rep", None, None, None, None),
    )
    out_specs = (P(("row", "rep"), None), P(), P())
    return jax.shard_map(shards, mesh=mesh, in_specs=in_specs, out_specs=out_specs, check_vma=False)
```

profile of v0, /device:TPU:0, one launch (start us, length us, event | category | flops | bytes accessed | tf_op | source)
XLA Modules:
  0.0 661.8 jit_solution(11847135036822304722)
XLA Ops:
  8.0 0.7 copy-done.4
  8.9 1.2 convolution_convert_fusion
  10.1 154.0 %while.38 = (s32[]{:T(128)}, bf16[2,256,256]{2,1,0:T(8,128)(2,1)S(1)}, s32[2]{0:T(128)S(1)}, s32[]{:T(128)}, bf16[256,256]{1,0:T(8,128)(2,1)S(1)}, /*index=5*/s32[]{:T(128)}, u32[]{:T(128)}, u32[]{:T(128)}) while((s32[]{:T(128)}, bf16[2,256,256]{2,1,0:T(8,128)(2,1)S(1)}, s32[2]{0:T(128)S(1)}, s32[]{:T(128)}, ...), condition=%wide.region_10.12_spmd, body=%wide.region_8.11_spmd.sunk | while | flops 131079 | bytes 1310923 | solution.py:25
  10.2 0.6 dynamic_slice.53
  11.4 0.7 select_bitcast_fusion.8
  12.1 75.9 %all-reduce.17.cloned.1.call-done = bf16[1,256,256]{2,1,0:T(8,128)(2,1)} async-done(((bf16[1,256,256]{2,1,0:T(8,128)(2,1)}), bf16[1,256,256]{2,1,0:T(8,128)(2,1)}) %all-reduce.17.cloned.1.call-update) | async-done | bytes 131088 | tf_op jit(solution)/shard_map/while/body/eval_jaxpr/psum | solution.py:9
  88.0 0.9 constant_dynamic-update-slice_fusion.8
  89.0 0.6 dynamic_slice.53
  90.2 0.7 select_bitcast_fusion.8
  90.9 72.3 %all-reduce.17.cloned.1.call-done = bf16[1,256,256]{2,1,0:T(8,128)(2,1)} async-done(((bf16[1,256,256]{2,1,0:T(8,128)(2,1)}), bf16[1,256,256]{2,1,0:T(8,128)(2,1)}) %all-reduce.17.cloned.1.call-update) | async-done | bytes 131088 | tf_op jit(solution)/shard_map/while/body/eval_jaxpr/psum | solution.py:9
  163.2 0.9 constant_dynamic-update-slice_fusion.8
  164.1 0.6 gather_fusion.2
  164.7 0.9 copy-done.1
  165.6 150.0 %while.36 = (s32[]{:T(128)}, bf16[2,256,256]{2,1,0:T(8,128)(2,1)S(1)}, s32[2]{0:T(128)S(1)}, s32[]{:T(128)}, bf16[256,256]{1,0:T(8,128)(2,1)S(1)}, /*index=5*/s32[]{:T(128)}, u32[]{:T(128)}, u32[]{:T(128)}) while((s32[]{:T(128)}, bf16[2,256,256]{2,1,0:T(8,128)(2,1)S(1)}, s32[2]{0:T(128)S(1)}, s32[]{:T(128)}, bf16[256,256]{1,0:T(8,128)(2,1)S(1)}, ...), condition=%wide.region_2.3_spmd, body=%wide.region_0.2_spmd.sunk | while | flops 131079 | bytes 1310923 | solution.py:25
  165.6 0.6 dynamic_slice.51
  166.8 0.7 select_bitcast_fusion.6
  167.5 72.3 %all-reduce.13.cloned.1.call-done = bf16[1,256,256]{2,1,0:T(8,128)(2,1)} async-done(((bf16[1,256,256]{2,1,0:T(8,128)(2,1)}), bf16[1,256,256]{2,1,0:T(8,128)(2,1)}) %all-reduce.13.cloned.1.call-update) | async-done | bytes 131088 | tf_op jit(solution)/shard_map/while/body/eval_jaxpr/psum | solution.py:9
  239.8 0.9 constant_dynamic-update-slice_fusion.6
  240.8 0.6 dynamic_slice.51
  242.1 0.7 select_bitcast_fusion.6
  242.8 71.9 %all-reduce.13.cloned.1.call-done = bf16[1,256,256]{2,1,0:T(8,128)(2,1)} async-done(((bf16[1,256,256]{2,1,0:T(8,128)(2,1)}), bf16[1,256,256]{2,1,0:T(8,128)(2,1)}) %all-reduce.13.cloned.1.call-update) | async-done | bytes 131088 | tf_op jit(solution)/shard_map/while/body/eval_jaxpr/psum | solution.py:9
  314.7 0.9 constant_dynamic-update-slice_fusion.6
  315.6 0.6 gather_fusion
  316.2 0.6 copy-done.6
  317.1 0.3 fusion.4
  317.4 13.1 %all-reduce.18 = bf16[256,256]{1,0:T(8,128)(2,1)S(1)} all-reduce(f32[256,256]{1,0:T(8,128)S(1)} %bitcast.65), channel_id=1, replica_groups=mesh['row'=8,'rep'=4] {'rep'}, use_global_device_ids=true, to_apply=%region_3.5 | all-reduce | flops 65536 | bytes 393216 | tf_op jit(solution)/shard_map/psum | solution.py:40
  330.5 1.0 fusion
  331.8 150.5 %while.37 = (s32[]{:T(128)}, bf16[2,256,256]{2,1,0:T(8,128)(2,1)S(1)}, s32[2]{0:T(128)S(1)}, s32[]{:T(128)}, bf16[256,256]{1,0:T(8,128)(2,1)S(1)}, /*index=5*/s32[]{:T(128)}, u32[]{:T(128)}, u32[]{:T(128)}) while((s32[]{:T(128)}, bf16[2,256,256]{2,1,0:T(8,128)(2,1)S(1)}, s32[2]{0:T(128)S(1)}, s32[]{:T(128)}, bf16[256,256]{1,0:T(8,128)(2,1)S(1)}, ...), condition=%wide.region_6.8_spmd, body=%wide.region_4.7_spmd.sunk | while | flops 131079 | bytes 1310923 | solution.py:25
  331.9 0.6 dynamic_slice.52
  333.1 0.7 select_bitcast_fusion.7
  333.8 72.7 %all-reduce.15.cloned.1.call-done = bf16[1,256,256]{2,1,0:T(8,128)(2,1)} async-done(((bf16[1,256,256]{2,1,0:T(8,128)(2,1)}), bf16[1,256,256]{2,1,0:T(8,128)(2,1)}) %all-reduce.15.cloned.1.call-update) | async-done | bytes 131088 | tf_op jit(solution)/shard_map/while/body/eval_jaxpr/psum | solution.py:9
  406.5 0.9 constant_dynamic-update-slice_fusion.7
  407.5 0.6 dynamic_slice.52
  408.8 0.7 select_bitcast_fusion.7
  409.5 71.9 %all-reduce.15.cloned.1.call-done = bf16[1,256,256]{2,1,0:T(8,128)(2,1)} async-done(((bf16[1,256,256]{2,1,0:T(8,128)(2,1)}), bf16[1,256,256]{2,1,0:T(8,128)(2,1)}) %all-reduce.15.cloned.1.call-update) | async-done | bytes 131088 | tf_op jit(solution)/shard_map/while/body/eval_jaxpr/psum | solution.py:9
  481.4 0.9 constant_dynamic-update-slice_fusion.7
  482.4 0.5 all-reduce.9.cloned.1.call-update
  483.0 0.6 gather_fusion.1
  483.7 0.3 fusion.2
  484.0 13.8 %all-reduce.19 = bf16[256,256]{1,0:T(8,128)(2,1)S(1)} all-reduce(f32[256,256]{1,0:T(8,128)S(1)} %bitcast.64), channel_id=1, replica_groups=mesh['row'=8,'rep'=4] {'rep'}, use_global_device_ids=true, to_apply=%region_7.9 | all-reduce | flops 65536 | bytes 393216 | tf_op jit(solution)/shard_map/psum | solution.py:40
  497.7 1.7 fusion.16
  499.4 17.9 %all-reduce.9.cloned.1.call-done = f32[256,256]{1,0:T(8,128)} async-done(((f32[256,256]{1,0:T(8,128)}), f32[256,256]{1,0:T(8,128)}) %all-reduce.9.cloned.1.call-update) | async-done | bytes 262160 | tf_op jit(solution)/shard_map/psum | solution.py:40
  517.3 1.8 fusion.15
  519.1 0.9 copy-done.2
  519.9 0.8 convolution_convert_fusion.1
  520.7 131.2 %all-reduce.11.cloned.1.call-done = (f32[256,256]{1,0:T(8,128)}, f32[256,256]{1,0:T(8,128)}) async-done(((f32[256,256]{1,0:T(8,128)}, f32[256,256]{1,0:T(8,128)}), (f32[256,256]{1,0:T(8,128)}, f32[256,256]{1,0:T(8,128)})) %all-reduce.11.cloned.1.call-update) | async-done | bytes 524304 | tf_op jit(solution)/shard_map/psum | solution.py:81
  651.9 1.7 copy.44
  653.6 0.7 copy.45
  (40 shorter events, 1.2 us)
Async XLA Ops:
  8.0 309.1 %copy-start = (bf16[1,1,2,4,128,128]{5,4,3,2,1,0:T(8,128)(2,1)S(1)}, bf16[1,1,2,4,128,128]{5,4,3,2,1,0:T(8,128)(2,1)}, u32[]{:S(2)}) copy-start(bf16[1,1,2,4,128,128]{5,4,3,2,1,0:T(8,128)(2,1)} %param.21) | copy-start | bytes 786436
  8.0 0.7 copy-start.4
  10.1 77.9 %all-reduce.17.cloned.1.call-start = ((), (), s32[]{:S(2)}) async-start(), calls=%async_computation.4 | async-start | bytes 262144 | tf_op jit(solution)/shard_map/while/body/eval_jaxpr/psum | solution.py:9
  88.9 74.3 %all-reduce.17.cloned.1.call-start = ((), (), s32[]{:S(2)}) async-start(), calls=%async_computation.4 | async-start | bytes 262144 | tf_op jit(solution)/shard_map/while/body/eval_jaxpr/psum | solution.py:9
  164.7 0.9 copy-start.1
  165.6 74.2 %all-reduce.13.cloned.1.call-start = ((), (), s32[]{:S(2)}) async-start(), calls=%async_computation.2 | async-start | bytes 262144 | tf_op jit(solution)/shard_map/while/body/eval_jaxpr/psum | solution.py:9
  240.8 73.9 %all-reduce.13.cloned.1.call-start = ((), (), s32[]{:S(2)}) async-start(), calls=%async_computation.2 | async-start | bytes 262144 | tf_op jit(solution)/shard_map/while/body/eval_jaxpr/psum | solution.py:9
  316.2 0.7 copy-start.6
  330.5 1.0 copy-start.5
  331.8 74.7 %all-reduce.15.cloned.1.call-start = ((), (), s32[]{:S(2)}) async-start(), calls=%async_computation.3 | async-start | bytes 262144 | tf_op jit(solution)/shard_map/while/body/eval_jaxpr/psum | solution.py:9
  407.5 73.9 %all-reduce.15.cloned.1.call-start = ((), (), s32[]{:S(2)}) async-start(), calls=%async_computation.3 | async-start | bytes 262144 | tf_op jit(solution)/shard_map/while/body/eval_jaxpr/psum | solution.py:9
  482.3 35.0 %all-reduce.9.cloned.1.call-start = ((), (), s32[]{:S(2)}) async-start(), calls=%async_computation | async-start | bytes 524288 | tf_op jit(solution)/shard_map/psum | solution.py:40
  482.9 169.0 %all-reduce.11.cloned.1.call-start = ((), (), s32[]{:S(2)}) async-start(), calls=%async_computation.1 | async-start | bytes 1048576 | tf_op jit(solution)/shard_map/psum | solution.py:81
  519.0 0.9 copy-start.2
  651.9 1.7 copy-start.3
Sparse Core Ops, SparseCore 0:
  14.8 73.1 all-reduce.16
  93.6 69.4 all-reduce.16
  170.3 69.4 all-reduce.12
  245.2 69.4 all-reduce.12
  336.2 70.2 all-reduce.14
  411.9 69.4 all-reduce.14
Sparse Core Ops, SparseCore 1:
  485.7 31.5 all-reduce.8
  523.2 128.7 all-reduce.10
where the time goes:
time: 662 us
  waiting for transfers between devices  587 us (89%)
  blocking collectives  26.8 us (4%)
  local copies, waits for them, and re-layouts  16.4 us (2%)
  between operations  15.7 us (2%)
  matrix products  7.22 us (1%)
    psum x6, waiting for transfers between devices, broadcast(): return lax.psum(jnp.where(mine, array, jnp.zeros_like(array)), axis)  437 us
    psum x1, waiting for transfers between devices, shards(): grad_one = lax.psum(grad_one, ('row', 'rep'))  131 us
    psum x2, blocking collectives, aggregate(): result = lax.psum(partial_value, 'rep')  26.8 us
    psum x1, waiting for transfers between devices, aggregate(): result = lax.psum(partial_value, 'rep')  17.9 us
  transfers between devices with their start and end apart: 8, of which 8 were waited for; matrix products, arithmetic and copies ran while one was open for 1% of the time, Pallas kernels for 0%

commit v1 on v0

--- a/solution.py
+++ b/solution.py
@@ -6,7 +6,10 @@
 
 def broadcast(array, axis, root):
     mine = lax.axis_index(axis) == root
-    return lax.psum(jnp.where(mine, array, jnp.zeros_like(array)), axis)
+    watch_layers_all = lambda my_tile, mesh_name: lax.all_gather(my_tile, axis_name=mesh_name).sum(
+        axis=0
+    )
+    return watch_layers_all(jnp.where(mine, array, jnp.zeros_like(array)), axis)
 
 
 def aggregate(source, block_index, block_count, block_values):

time: 662 us -> 475 us (0.72)
  waiting for transfers between devices: 587 us -> 397 us
  other arithmetic: 4.38 us -> 12.6 us
    psum x6 -> x0, waiting for transfers between devices: 437 us -> none  [broadcast(): return lax.psum(jnp.where(mine, array, jnp.zeros_like(array)), axis)]
    all_gather x0 -> x6, waiting for transfers between devices: none -> 247 us  [broadcast(): lax.all_gather(my_tile, axis_name=mesh_name).sum(axis=0)]
    reduce_sum x0 -> x6, other arithmetic: none -> 8.23 us  [broadcast(): lax.all_gather(my_tile, axis_name=mesh_name).sum(axis=0)]
where the time goes in v1:
time: 475 us; the launch traced here: 474 us
  waiting for transfers between devices  397 us (84%)
  blocking collectives  26.6 us (6%)
  between operations  15.7 us (3%)
  other arithmetic  12.6 us (3%)
  local copies, waits for them, and re-layouts  11.1 us (2%)
  matrix products  7.22 us (2%)
    all_gather x6, waiting for transfers between devices, broadcast(): lax.all_gather(my_tile, axis_name=mesh_name).sum(axis=0)  247 us
    psum x1, waiting for transfers between devices, shards(): grad_one = lax.psum(grad_one, ('row', 'rep'))  131 us
    psum x2, blocking collectives, aggregate(): result = lax.psum(partial_value, 'rep')  26.6 us
    psum x1, waiting for transfers between devices, aggregate(): result = lax.psum(partial_value, 'rep')  17.7 us
  transfers between devices with their start and end apart: 8, of which 8 were waited for; matrix products, arithmetic and copies ran while one was open for 1% of the time, Pallas kernels for 0%

profile of v1, /device:TPU:0, one launch (start us, length us, event | category | flops | bytes accessed | tf_op | source)
XLA Modules:
  0.0 474.4 jit_solution(16748170341607834419)
XLA Ops:
  8.0 0.7 copy-done.4
  8.9 1.2 convolution_convert_fusion
  10.1 91.9 %while.38 = (s32[]{:T(128)}, bf16[2,256,256]{2,1,0:T(8,128)(2,1)S(1)}, s32[2]{0:T(128)S(1)}, s32[]{:T(128)}, bf16[256,256]{1,0:T(8,128)(2,1)S(1)}, /*index=5*/s32[]{:T(128)}, u32[]{:T(128)}, u32[]{:T(128)}, bf16[]{:T(256)}) while((s32[]{:T(128)}, bf16[2,256,256]{2,1,0:T(8,128)(2,1)S(1)}, s32[2]{0:T(128)S(1)}, s32[]{:T(128)}, ...), condition=%wide.region_10.12_spmd, body=%wide.region_8.11_spmd.sunk | while | flops 524295 | bytes 5243093 | solution.py:28
  10.2 0.6 dynamic_slice.56
  11.4 0.7 broadcast_select_fusion.11
  12.1 44.6 %all-gather.17.cloned.1.call-done = bf16[2048,256]{1,0:T(8,128)(2,1)} async-done(((bf16[256,256]{1,0:T(8,128)(2,1)}), bf16[2048,256]{1,0:T(8,128)(2,1)}) %all-gather.17.cloned.1.call-update) | async-done | bytes 1048592 | tf_op jit(solution)/shard_map/while/body/eval_jaxpr/all_gather | solution.py:9
  56.6 1.4 reduce_sum.41
  58.1 0.6 dynamic_slice.56
  59.4 0.7 broadcast_select_fusion.11
  60.1 40.5 %all-gather.17.cloned.1.call-done = bf16[2048,256]{1,0:T(8,128)(2,1)} async-done(((bf16[256,256]{1,0:T(8,128)(2,1)}), bf16[2048,256]{1,0:T(8,128)(2,1)}) %all-gather.17.cloned.1.call-update) | async-done | bytes 1048592 | tf_op jit(solution)/shard_map/while/body/eval_jaxpr/all_gather | solution.py:9
  100.6 1.4 reduce_sum.41
  102.0 0.6 gather_fusion.2
  102.6 0.9 copy-done.1
  103.5 87.6 %while.36 = (s32[]{:T(128)}, bf16[2,256,256]{2,1,0:T(8,128)(2,1)S(1)}, s32[2]{0:T(128)S(1)}, s32[]{:T(128)}, bf16[256,256]{1,0:T(8,128)(2,1)S(1)}, /*index=5*/s32[]{:T(128)}, u32[]{:T(128)}, u32[]{:T(128)}, bf16[]{:T(256)}) while((s32[]{:T(128)}, bf16[2,256,256]{2,1,0:T(8,128)(2,1)S(1)}, s32[2]{0:T(128)S(1)}, s32[]{:T(128)}, ...), condition=%wide.region_2.3_spmd, body=%wide.region_0.2_spmd.sunk | while | flops 524295 | bytes 5243093 | solution.py:28
  103.5 0.6 dynamic_slice.54
  104.8 0.7 broadcast_select_fusion.9
  105.5 40.6 %all-gather.13.cloned.1.call-done = bf16[2048,256]{1,0:T(8,128)(2,1)} async-done(((bf16[256,256]{1,0:T(8,128)(2,1)}), bf16[2048,256]{1,0:T(8,128)(2,1)}) %all-gather.13.cloned.1.call-update) | async-done | bytes 1048592 | tf_op jit(solution)/shard_map/while/body/eval_jaxpr/all_gather | solution.py:9
  146.0 1.4 reduce_sum.39
  147.5 0.6 dynamic_slice.54
  148.7 0.7 broadcast_select_fusion.9
  149.4 40.2 %all-gather.13.cloned.1.call-done = bf16[2048,256]{1,0:T(8,128)(2,1)} async-done(((bf16[256,256]{1,0:T(8,128)(2,1)}), bf16[2048,256]{1,0:T(8,128)(2,1)}) %all-gather.13.cloned.1.call-update) | async-done | bytes 1048592 | tf_op jit(solution)/shard_map/while/body/eval_jaxpr/all_gather | solution.py:9
  189.7 1.4 reduce_sum.39
  191.1 0.6 gather_fusion
  191.7 0.6 copy-done.6
  192.6 0.3 fusion.4
  192.9 13.1 %all-reduce.9 = bf16[256,256]{1,0:T(8,128)(2,1)S(1)} all-reduce(f32[256,256]{1,0:T(8,128)S(1)} %bitcast.77), channel_id=1, replica_groups=mesh['row'=8,'rep'=4] {'rep'}, use_global_device_ids=true, to_apply=%region_3.5 | all-reduce | flops 65536 | bytes 393216 | tf_op jit(solution)/shard_map/psum | solution.py:43
  206.0 1.0 fusion
  207.2 88.1 %while.37 = (s32[]{:T(128)}, bf16[2,256,256]{2,1,0:T(8,128)(2,1)S(1)}, s32[2]{0:T(128)S(1)}, s32[]{:T(128)}, bf16[256,256]{1,0:T(8,128)(2,1)S(1)}, /*index=5*/s32[]{:T(128)}, u32[]{:T(128)}, u32[]{:T(128)}, bf16[]{:T(256)}) while((s32[]{:T(128)}, bf16[2,256,256]{2,1,0:T(8,128)(2,1)S(1)}, s32[2]{0:T(128)S(1)}, s32[]{:T(128)}, ...), condition=%wide.region_6.8_spmd, body=%wide.region_4.7_spmd.sunk | while | flops 524295 | bytes 5243093 | solution.py:28
  207.3 0.6 dynamic_slice.55
  208.5 0.7 broadcast_select_fusion.10
  209.2 41.0 %all-gather.15.cloned.1.call-done = bf16[2048,256]{1,0:T(8,128)(2,1)} async-done(((bf16[256,256]{1,0:T(8,128)(2,1)}), bf16[2048,256]{1,0:T(8,128)(2,1)}) %all-gather.15.cloned.1.call-update) | async-done | bytes 1048592 | tf_op jit(solution)/shard_map/while/body/eval_jaxpr/all_gather | solution.py:9
  250.3 1.4 reduce_sum.40
  251.7 0.6 dynamic_slice.55
  253.0 0.7 broadcast_select_fusion.10
  253.7 40.2 %all-gather.15.cloned.1.call-done = bf16[2048,256]{1,0:T(8,128)(2,1)} async-done(((bf16[256,256]{1,0:T(8,128)(2,1)}), bf16[2048,256]{1,0:T(8,128)(2,1)}) %all-gather.15.cloned.1.call-update) | async-done | bytes 1048592 | tf_op jit(solution)/shard_map/while/body/eval_jaxpr/all_gather | solution.py:9
  293.9 1.4 reduce_sum.40
  295.3 0.5 all-reduce.6.cloned.1.call-update
  295.9 0.6 gather_fusion.1
  296.6 0.3 fusion.2
  296.9 13.5 %all-reduce.10 = bf16[256,256]{1,0:T(8,128)(2,1)S(1)} all-reduce(f32[256,256]{1,0:T(8,128)S(1)} %bitcast.76), channel_id=1, replica_groups=mesh['row'=8,'rep'=4] {'rep'}, use_global_device_ids=true, to_apply=%region_7.9 | all-reduce | flops 65536 | bytes 393216 | tf_op jit(solution)/shard_map/psum | solution.py:43
  310.5 1.7 fusion.16
  312.2 17.7 %all-reduce.6.cloned.1.call-done = f32[256,256]{1,0:T(8,128)} async-done(((f32[256,256]{1,0:T(8,128)}), f32[256,256]{1,0:T(8,128)}) %all-reduce.6.cloned.1.call-update) | async-done | bytes 262160 | tf_op jit(solution)/shard_map/psum | solution.py:43
  329.9 1.8 fusion.15
  331.7 0.9 copy-done.2
  332.5 0.8 convolution_convert_fusion.1
  333.3 131.2 %all-reduce.8.cloned.1.call-done = (f32[256,256]{1,0:T(8,128)}, f32[256,256]{1,0:T(8,128)}) async-done(((f32[256,256]{1,0:T(8,128)}, f32[256,256]{1,0:T(8,128)}), (f32[256,256]{1,0:T(8,128)}, f32[256,256]{1,0:T(8,128)})) %all-reduce.8.cloned.1.call-update) | async-done | bytes 524304 | tf_op jit(solution)/shard_map/psum | solution.py:84
  464.5 1.7 copy.44
  466.2 0.7 copy.45
  (46 shorter events, 1.3 us)
Async XLA Ops:
  8.0 184.6 %copy-start = (bf16[1,1,2,4,128,128]{5,4,3,2,1,0:T(8,128)(2,1)S(1)}, bf16[1,1,2,4,128,128]{5,4,3,2,1,0:T(8,128)(2,1)}, u32[]{:S(2)}) copy-start(bf16[1,1,2,4,128,128]{5,4,3,2,1,0:T(8,128)(2,1)} %param.21) | copy-start | bytes 786436
  8.0 0.7 copy-start.4
  10.1 46.6 %all-gather.17.cloned.1.call-start = ((), (), s32[]{:S(2)}) async-start(), calls=%async_computation.4 | async-start | bytes 1179648 | tf_op jit(solution)/shard_map/while/body/eval_jaxpr/all_gather | solution.py:9
  58.1 42.5 %all-gather.17.cloned.1.call-start = ((), (), s32[]{:S(2)}) async-start(), calls=%async_computation.4 | async-start | bytes 1179648 | tf_op jit(solution)/shard_map/while/body/eval_jaxpr/all_gather | solution.py:9
  102.6 0.9 copy-start.1
  103.5 42.5 %all-gather.13.cloned.1.call-start = ((), (), s32[]{:S(2)}) async-start(), calls=%async_computation.2 | async-start | bytes 1179648 | tf_op jit(solution)/shard_map/while/body/eval_jaxpr/all_gather | solution.py:9
  147.4 42.2 %all-gather.13.cloned.1.call-start = ((), (), s32[]{:S(2)}) async-start(), calls=%async_computation.2 | async-start | bytes 1179648 | tf_op jit(solution)/shard_map/while/body/eval_jaxpr/all_gather | solution.py:9
  191.7 0.7 copy-start.6
  205.9 1.0 copy-start.5
  207.2 43.0 %all-gather.15.cloned.1.call-start = ((), (), s32[]{:S(2)}) async-start(), calls=%async_computation.3 | async-start | bytes 1179648 | tf_op jit(solution)/shard_map/while/body/eval_jaxpr/all_gather | solution.py:9
  251.7 42.2 %all-gather.15.cloned.1.call-start = ((), (), s32[]{:S(2)}) async-start(), calls=%async_computation.3 | async-start | bytes 1179648 | tf_op jit(solution)/shard_map/while/body/eval_jaxpr/all_gather | solution.py:9
  295.3 34.6 %all-reduce.6.cloned.1.call-start = ((), (), s32[]{:S(2)}) async-start(), calls=%async_computation | async-start | bytes 524288 | tf_op jit(solution)/shard_map/psum | solution.py:43
  295.9 168.6 %all-reduce.8.cloned.1.call-start = ((), (), s32[]{:S(2)}) async-start(), calls=%async_computation.1 | async-start | bytes 1048576 | tf_op jit(solution)/shard_map/psum | solution.py:84
  331.6 0.9 copy-start.2
  464.5 1.7 copy-start.3
Sparse Core Ops, SparseCore 0:
  13.6 42.9 all-gather.16
  61.6 38.9 all-gather.16
  107.0 38.9 all-gather.12
  150.6 38.9 all-gather.12
  210.5 39.7 all-gather.14
  254.9 38.9 all-gather.14
Sparse Core Ops, SparseCore 1:
  298.7 31.1 all-reduce.5
  335.8 128.7 all-reduce.7
